TPU v7x, 256 devices: a whole 4x4x8 slice. The times are simulated.
256 devices in a mesh: ctx: 16 (over x, y_hi, core), tp: 16 (over z, y_lo).
Axes of the slice: x: 4, y: 4 (y_hi: 2, y_lo: 2; y = y_hi * 2 + y_lo), z: 8, core: 2. Of those that a mesh axis runs over, the one named last changes fastest.
Arguments:
- tokens: bfloat16 [2048, 4096], P('ctx', 'tp'), may hold values from -6 to 6
- gate_tiles: bfloat16 [1024, 128, 128], P('tp'), may hold values from -0.25 to 0.25
- up_tiles: bfloat16 [1024, 128, 128], P('tp'), may hold values from -0.25 to 0.25
- down_tiles: bfloat16 [1024, 128, 128], P('tp'), may hold values from -0.125 to 0.125
- gu_blocks: int32 [2, 1024], P(None, 'tp'), may hold values from 0 to 31, as said below
- down_blocks: int32 [2, 1024], P(None, 'tp'), may hold values from 0 to 31, as said below
- counts: int32 [2, 16], P(None, 'tp'), may hold values from 1 to 64, as said below
Outputs:
- mixed: bfloat16 [128, 16, 4096], P('tp', None, 'ctx')
Inputs may be any that keep to these rules, and one draw needn't show every extreme that they name: `gu_blocks`: within one shard's 64 slots the pairs (row 0, row 1) are all different; row 0 is below 32, row 1 below 8. `down_blocks`: within one shard's 64 slots the pairs (row 0, row 1) are all different; row 0 is below 8, row 1 below 32. In each row some shard has exactly 64 live slots; only the first counts slots of a shard are live.
All inputs are finite; a program needn't handle non-finite values.
Results may differ from a plain program's by a relative error of at most 0.0052.
Values may be sent and summed in bfloat16 or wider, within the bound.
No kernel may reach another device: no remote copies, remote signals or barrier semaphores. Data moves between devices by JAX's collectives and lax.ppermute only.
A program may use at most 64 MiB of HBM per device.

v0:
```python
import jax
import jax.numpy as jnp
from jax import lax
from jax.sharding import PartitionSpec as P

FF = 16384


def per_device(tokens, gate_tiles, up_tiles, down_tiles, gu_blocks, down_blocks, counts):
    gathered = lax.all_gather(tokens, "tp", axis=1, tiled=True)
    tok_rows, feat_width = gathered.shape
    slot_count = gate_tiles.shape[0]
    tile_size = gate_tiles.shape[1]
    in_blocks = feat_width // tile_size
    tp_count = lax.axis_size("tp")
    hid_blocks = FF // tp_count // tile_size
    widened = gathered.astype(jnp.float32)
    squares = jnp.mean(widened * widened, axis=1, keepdims=True)
    normed = (widened * lax.rsqrt(squares + 1e-05)).astype(jnp.bfloat16)
    slot_ids = jnp.arange(slot_count)
    valid_in = (slot_ids < counts[0, 0]).astype(jnp.float32)
    valid_out = (slot_ids < counts[1, 0]).astype(jnp.float32)
    pick_hidden = (gu_blocks[1][:, None] == jnp.arange(hid_blocks)[None, :]).astype(
        jnp.float32
    ) * valid_in[:, None]
    pick_out = (down_blocks[1][:, None] == jnp.arange(in_blocks)[None, :]).astype(
        jnp.float32
    ) * valid_out[:, None]
    block_rows = min(tok_rows, 512)

    def hidden_block(row_block):
        row_tiles = row_block.reshape(block_rows, in_blocks, tile_size)
        chosen = jnp.take(row_tiles, gu_blocks[0], axis=1)
        gate_part = jnp.einsum(
            "tmk,mkn->tmn", chosen, gate_tiles, preferred_element_type=jnp.float32
        )
        up_part = jnp.einsum("tmk,mkn->tmn", chosen, up_tiles, preferred_element_type=jnp.float32)
        gate_sum = jnp.einsum(
            "tmn,mh->thn", gate_part, pick_hidden, precision=lax.Precision.HIGHEST
        )
        up_sum = jnp.einsum("tmn,mh->thn", up_part, pick_hidden, precision=lax.Precision.HIGHEST)
        return (jax.nn.silu(gate_sum) * up_sum).astype(jnp.bfloat16)

    hidden = lax.map(hidden_block, normed.reshape(tok_rows // block_rows, block_rows, feat_width))
    hidden = hidden.reshape(tok_rows, hid_blocks, tile_size)
    first_shard = jnp.where(lax.axis_index("tp") == 0, 1.0, 0.0).astype(jnp.float32)
    chosen_hidden = jnp.take(hidden, down_blocks[0], axis=1)
    products = jnp.einsum(
        "tmk,mkn->tmn", chosen_hidden, down_tiles, preferred_element_type=jnp.float32
    )
    summed = jnp.einsum("tmn,mo->ton", products, pick_out, precision=lax.Precision.HIGHEST)
    partial_term = summed.reshape(tok_rows, feat_width) + first_shard * widened
    arrived = lax.all_to_all(
        partial_term.reshape(tok_rows, 1, feat_width),
        "ctx",
        split_axis=2,
        concat_axis=1,
        tiled=True,
    )
    finished = lax.psum_scatter(arrived, "tp", scatter_dimension=0, tiled=True)
    return finished.astype(jnp.bfloat16)


def solution(mesh):
    return jax.shard_map(
        per_device,
        mesh=mesh,
        in_specs=(
            P("ctx", "tp"),
            P("tp", None, None),
            P("tp", None, None),
            P("tp", None, None),
            P(None, "tp"),
            P(None, "tp"),
            P(None, "tp"),
        ),
        out_specs=P("tp", None, "ctx"),
        check_vma=False,
    )
```

profile of v0, /device:TPU:2, one launch (start us, length us, event | category | flops | bytes accessed | tf_op | source)
XLA Modules:
  0.0 236.4 jit_solution(7079399391941856147)
XLA Ops:
  6.5 0.0 copy-start
  6.5 0.0 all-gather.2.cloned.1.call-start
  6.5 1.7 copy.17
  8.3 0.0 all-gather.2.cloned.1.call-update
  8.3 0.0 reduce-scatter.2.cloned.1.call-start
  8.3 1.3 fusion.53
  9.7 0.7 compare_convert_fusion
  10.4 0.6 compare_convert_fusion.1
  10.9 0.7 fusion.45
  11.6 0.7 fusion.46
  12.3 0.7 compare_and_fusion
  13.0 0.7 slice_bitcast_fusion
  13.7 0.7 compare_and_fusion.1
  14.4 0.7 slice_bitcast_fusion.1
  15.1 65.7 %all-gather.2.cloned.1.call-done = bf16[128,4096]{0,1:T(8,128)(2,1)} async-done(((bf16[128,256]{0,1:T(8,128)(2,1)}), bf16[128,4096]{0,1:T(8,128)(2,1)}) %all-gather.2.cloned.1.call-update) | async-done | bytes 1048592 | tf_op jit(solution)/shard_map/all_gather | solution.py:10
  80.8 1.8 fusion.6
  82.6 2.4 %fusion.7 = bf16[128,4096]{0,1:T(8,128)(2,1)} fusion(bf16[128,4096]{0,1:T(8,128)(2,1)} %all-gather.2.cloned.1.call-done, f32[128]{0:T(128)S(1)} %add_rsqrt_fusion), kind=kLoop, calls=%fused_computation.15 | loop fusion | flops 1572864 | bytes 2097664 | tf_op jit(solution)/shard_map/convert_element_type | solution.py:19
  85.0 1.6 copy.18
  86.6 2.2 gather_fusion
  88.8 0.0 copy-done
  88.8 0.0 copy-start.1
  88.8 0.0 copy-start.3
  88.8 2.5 %convolution_bitcast_fusion.2 = f32[128,64,128]{2,0,1:T(8,128)S(1)} fusion(bf16[64,128,128]{2,1,0:T(8,128)(2,1)S(1)} %copy-done, bf16[64,128,128]{2,1,0:T(8,128)(2,1)} %gather_fusion, pred[64]{0:T(512)(128)(4,1)S(1)} %compare_and_fusion), kind=kOutput, calls=%fused_computation.13 | convolution fusion | flops 269484032 | bytes 8388672 | tf_op jit(solution)/shard_map/while/body/eval_jaxpr/tmk,mkn->tmn/dot_general | solution.py:34
  91.3 0.0 copy-done.1
  91.3 0.3 copy-done.3
  91.6 0.8 convolution_bitcast_fusion.1
  92.4 4.4 %fusion.17 = f32[128,8,128]{2,1,0:T(8,128)S(1)} fusion(f32[128,64,128]{2,0,1:T(8,128)S(1)} %convolution_bitcast_fusion.2, f32[64]{0:T(128)S(1)} %compare_convert_fusion, s32[64]{0:T(128)S(1)} %slice_bitcast_fusion), kind=kOutput, calls=%fused_computation.24 | convolution fusion | flops 100664320 | bytes 4719104 | tf_op jit(solution)/shard_map/while/body/eval_jaxpr/tmn,mh->thn/dot_general | solution.py:38
  96.8 4.4 %fusion.26 = bf16[128,8,128]{2,1,0:T(8,128)(2,1)S(1)} fusion(f32[128,64,128]{2,0,1:T(8,128)S(1)} %convolution_bitcast_fusion.1, f32[128,8,128]{2,1,0:T(8,128)S(1)} %fusion.17, f32[64]{0:T(128)S(1)} %compare_convert_fusion, s32[64]{0:T(128)S(1)} %slice_bitcast_fusion), kind=kOutput, calls=%fused_computation.27 | convolution fusion | flops 101450752 | bytes 4981248 | tf_op jit(solution)/shard_map/while/body/eval_jaxpr/tmn,mh->thn/dot_general | solution.py:41
  101.2 2.2 gather_fusion.1
  103.3 3.0 %convolution_bitcast_fusion = f32[128,64,128]{2,0,1:T(8,128)S(1)} fusion(bf16[64,128,128]{2,1,0:T(8,128)(2,1)} %param.10, bf16[64,128,128]{2,1,0:T(8,128)(2,1)} %gather_fusion.1, pred[64]{0:T(512)(128)(4,1)S(1)} %compare_and_fusion.1), kind=kOutput, calls=%fused_computation.11 | convolution fusion | flops 269484032 | bytes 8388672 | tf_op jit(solution)/shard_map/tmk,mkn->tmn/dot_general | solution.py:48
  106.3 6.0 %fusion.14 = f32[128,32,128]{2,1,0:T(8,128)} fusion(f32[128,64,128]{2,0,1:T(8,128)S(1)} %convolution_bitcast_fusion, f32[64]{0:T(128)S(1)} %compare_convert_fusion.1, s32[64]{0:T(128)S(1)} %slice_bitcast_fusion.1), kind=kOutput, calls=%fused_computation.23 | convolution fusion | flops 402657280 | bytes 6291968 | tf_op jit(solution)/shard_map/tmn,mo->ton/dot_general | solution.py:51
  112.3 0.0 copy-start.2
  112.3 3.1 %copy.26 = f32[128,32,128]{0,2,1:T(8,128)} copy(f32[128,32,128]{2,1,0:T(8,128)} %fusion.14) | data formatting | bytes 4194304 | tf_op jit(solution)/shard_map/reshape | solution.py:52
  115.4 0.0 copy-done.2
  115.4 1.8 fusion.8
  117.2 33.9 %all_to_all.12 = f32[128,1,4096]{0,1,2:T(1,128)} all-to-all(f32[128,1,4096]{0,1,2:T(1,128)S(1)} %bitcast.60), channel_id=1, replica_groups=mesh['ctx'=16,'tp'=16] {'ctx'}, dimensions={2} | all-to-all | bytes 4194304 | tf_op jit(solution)/shard_map/all_to_all | solution.py:53
  151.1 3.1 %copy.25 = f32[128,16,256]{2,1,0:T(8,128)} copy(f32[128,16,256]{0,2,1:T(8,128)} %bitcast.61) | data formatting | bytes 4194304 | tf_op jit(solution)/shard_map/all_to_all | solution.py:53
  154.2 0.0 reduce-scatter.2.cloned.1.call-update
  154.2 73.8 %reduce-scatter.2.cloned.1.call-done = f32[8,16,256]{2,1,0:T(8,128)} async-done(((f32[128,16,256]{2,1,0:T(8,128)}), f32[8,16,256]{2,1,0:T(8,128)}) %reduce-scatter.2.cloned.1.call-update) | async-done | bytes 131088 | tf_op jit(solution)/shard_map/reduce_scatter | solution.py:60
  228.0 1.5 convert_element_type.34
  (4 shorter events, 0.1 us)
Async XLA Ops:
  6.5 82.2 %copy-start = (bf16[64,128,128]{2,1,0:T(8,128)(2,1)S(1)}, bf16[64,128,128]{2,1,0:T(8,128)(2,1)}, u32[]{:S(2)}) copy-start(bf16[64,128,128]{2,1,0:T(8,128)(2,1)} %param.8) | copy-start | bytes 6291460
  6.5 74.2 %all-gather.2.cloned.1.call-start = ((), (), s32[]{:S(2)}) async-start(), calls=%async_computation.2 | async-start | bytes 1114112 | tf_op jit(solution)/shard_map/all_gather | solution.py:10
  8.3 219.7 %reduce-scatter.2.cloned.1.call-start = ((), (), s32[]{:S(2)}) async-start(), calls=%async_computation.3 | async-start | bytes 2228224 | tf_op jit(solution)/shard_map/reduce_scatter | solution.py:60
  88.8 2.5 %copy-start.1 = (bf16[64,128,128]{2,1,0:T(8,128)(2,1)S(1)}, bf16[64,128,128]{2,1,0:T(8,128)(2,1)}, u32[]{:S(2)}) copy-start(bf16[64,128,128]{2,1,0:T(8,128)(2,1)} %gather_fusion) | copy-start | bytes 6291460
  88.8 2.9 %copy-start.3 = (bf16[64,128,128]{2,1,0:T(8,128)(2,1)S(1)}, bf16[64,128,128]{2,1,0:T(8,128)(2,1)}, u32[]{:S(2)}) copy-start(bf16[64,128,128]{2,1,0:T(8,128)(2,1)} %param.9) | copy-start | bytes 6291460
  112.3 3.1 %copy-start.2 = (bf16[128,4096]{0,1:T(8,128)(2,1)S(1)}, bf16[128,4096]{0,1:T(8,128)(2,1)}, u32[]{:S(2)}) copy-start(bf16[128,4096]{0,1:T(8,128)(2,1)} %all-gather.2.cloned.1.call-done) | copy-start | bytes 3145732
Sparse Core Ops, SparseCore 0:
  9.1 71.5 all-gather.1
  154.4 73.5 reduce-scatter.1
where the time goes:
time: 237 us; the launch traced here: 236 us
  waiting for transfers between devices  140 us (59%)
  blocking collectives  33.9 us (14%)
  matrix products  21 us (9%)
  local copies, waits for them, and re-layouts  16.9 us (7%)
  between operations  13.5 us (6%)
  other arithmetic  11.5 us (5%)
    reduce_scatter x1, waiting for transfers between devices, per_device(): finished = lax.psum_scatter(arrived, 'tp', scatter_dimension=0, tiled=True)  73.8 us
    all_gather x1, waiting for transfers between devices, per_device(): gathered = lax.all_gather(tokens, 'tp', axis=1, tiled=True)  65.7 us
    all_to_all x1, blocking collectives, per_device(): lax.all_to_all(partial_term.reshape(tok_rows, 1, feat_width), 'ctx', spli...  33.9 us
    dot_general x1, matrix products, per_device(): jnp.einsum('tmn,mo->ton', products, pick_out, precision=lax.Precision.HIG...  6 us
  transfers between devices with their start and end apart: 2, of which 2 were waited for; matrix products, arithmetic and copies ran while one was open for 3% of the time, Pallas kernels for 0%

commit v1 on v0

--- a/solution.py
+++ b/solution.py
@@ -7,7 +7,9 @@
 
 
 def per_device(tokens, gate_tiles, up_tiles, down_tiles, gu_blocks, down_blocks, counts):
-    gathered = lax.all_gather(tokens, "tp", axis=1, tiled=True)
+    gathered = jnp.concatenate(
+        lax.all_to_all(jnp.stack([tokens] * lax.axis_size("tp")), "tp", 0, 0), axis=1
+    )
     tok_rows, feat_width = gathered.shape
     slot_count = gate_tiles.shape[0]
     tile_size = gate_tiles.shape[1]

time: 237 us -> 212 us (0.89)
  waiting for transfers between devices: 140 us -> 96.6 us
  starting transfers between devices: 0.04 us -> 9.62 us
  local copies, waits for them, and re-layouts: 16.9 us -> 24.8 us
    all_gather x1 -> x0, waiting for transfers between devices: 65.7 us -> none  [per_device(): gathered = lax.all_gather(tokens, 'tp', axis=1, tiled=True)]
    all_to_all x0 -> x1, waiting for transfers between devices: none -> 26.6 us  [per_device(): lax.all_to_all(jnp.stack([tokens] * lax.axis_size('tp')), 'tp', 0, 0)]
    all_to_all x0 -> x1, starting transfers between devices: none -> 9.58 us  [per_device(): lax.all_to_all(jnp.stack([tokens] * lax.axis_size('tp')), 'tp', 0, 0)]
    add x0 -> x1, local copies, waits for them, and re-layouts: none -> 5.63 us  [per_device(): partial_term = summed.reshape(tok_rows, feat_width) + first_shard * widened]
    reduce_scatter x1, waiting for transfers between devices: 73.8 us -> 70 us  [per_device(): finished = lax.psum_scatter(arrived, 'tp', scatter_dimension=0, tiled=True)]
    convert_element_type x0 -> x1, local copies, waits for them, and re-layouts: none -> 2.92 us  [per_device(): widened = gathered.astype(jnp.float32)]
    mul x0 -> x1, local copies, waits for them, and re-layouts: none -> 2.92 us  [per_device(): partial_term = summed.reshape(tok_rows, feat_width) + first_shard * widened]
  transfers between devices with their start and end apart: 2 -> 2, of which waited for: 2 -> 2; matrix products, arithmetic and copies ran while one was open for 3% -> 1% of each run, Pallas kernels for 0% -> 0%
where the time goes in v1:
time: 212 us
  waiting for transfers between devices  96.6 us (46%)
  blocking collectives  34.1 us (16%)
  local copies, waits for them, and re-layouts  24.8 us (12%)
  matrix products  21 us (10%)
  between operations  13.6 us (6%)
  other arithmetic  11.9 us (6%)
  starting transfers between devices  9.62 us (5%)
    reduce_scatter x1, waiting for transfers between devices, per_device(): finished = lax.psum_scatter(arrived, 'tp', scatter_dimension=0, tiled=True)  70 us
    all_to_all x1, blocking collectives, per_device(): lax.all_to_all(partial_term.reshape(tok_rows, 1, feat_width), 'ctx', spli...  34.1 us
    all_to_all x1, waiting for transfers between devices, per_device(): lax.all_to_all(jnp.stack([tokens] * lax.axis_size('tp')), 'tp', 0, 0)  26.6 us
    all_to_all x1, starting transfers between devices, per_device(): lax.all_to_all(jnp.stack([tokens] * lax.axis_size('tp')), 'tp', 0, 0)  9.58 us
    dot_general x1, matrix products, per_device(): jnp.einsum('tmn,mo->ton', products, pick_out, precision=lax.Precision.HIG...  6.04 us
    add x1, local copies, waits for them, and re-layouts, per_device(): partial_term = summed.reshape(tok_rows, feat_width) + first_shard * widened  5.63 us
    dot_general x1, matrix products, hidden_block(): jnp.einsum('tmn,mh->thn', gate_part, pick_hidden, precision=lax.Precision...  4.37 us
    dot_general x1, matrix products, hidden_block(): jnp.einsum('tmn,mh->thn', up_part, pick_hidden, precision=lax.Precision.H...  4.36 us
  transfers between devices with their start and end apart: 2, of which 2 were waited for; matrix products, arithmetic and copies ran while one was open for 1% of the time, Pallas kernels for 0%

profile of v1, /device:TPU:2, one launch (start us, length us, event | category | flops | bytes accessed | tf_op | source)
XLA Modules:
  0.0 211.7 jit_solution(6531631444712358306)
XLA Ops:
  6.5 0.0 copy-start
  6.5 0.0 copy-start.3
  6.5 0.0 copy-start.4
  6.5 0.0 copy-start.5
  6.5 1.1 copy.25
  7.6 1.2 stack.2
  8.8 9.6 %all-to-all-start = ((bf16[16,128,256]{1,2,0:T(8,128)(2,1)}), bf16[16,128,256]{1,2,0:T(8,128)(2,1)S(1)}, u32[]{:S(2)}, u32[]{:S(2)}) async-start(bf16[16,128,256]{1,2,0:T(8,128)(2,1)} %stack.2), calls=%async_computation | async-start | bytes 2097152 | tf_op jit(solution)/shard_map/all_to_all | solution.py:11
  18.4 0.0 reduce-scatter.2.cloned.1.call-start
  18.5 0.0 copy-done.3
  18.5 0.6 fusion.50
  19.1 0.6 compare_convert_fusion
  19.7 0.7 compare_convert_fusion.1
  20.4 0.0 copy-done.4
  20.4 0.0 copy-done.5
  20.5 26.6 %all-to-all-done = bf16[16,128,256]{1,2,0:T(8,128)(2,1)S(1)} async-done(((bf16[16,128,256]{1,2,0:T(8,128)(2,1)}), bf16[16,128,256]{1,2,0:T(8,128)(2,1)S(1)}, u32[]{:S(2)}, u32[]{:S(2)}) %all-to-all-start) | async-done | bytes 1048608 | tf_op jit(solution)/shard_map/all_to_all | solution.py:11
  47.1 1.8 convert_multiply_fusion
  48.9 1.5 convert_element_type.60
  50.4 2.9 %copy.26 = f32[128,32,128]{2,0,1:T(8,128)} copy(f32[128,32,128]{0,2,1:T(8,128)} %bitcast.61) | data formatting | bytes 4194304 | tf_op jit(solution)/shard_map/convert_element_type | solution.py:19
  53.4 1.9 multiply_convert_fusion
  55.3 2.1 %gather_fusion = bf16[64,128,128]{2,1,0:T(8,128)(2,1)} fusion(bf16[128,32,128]{2,0,1:T(8,128)(2,1)S(1)} %multiply_convert_fusion, s32[1024]{0:T(1024)S(1)} %pad_clamp_fusion.1), kind=kCustom, calls=%fused_computation | custom fusion | bytes 4194560 | tf_op jit(solution)/shard_map/while/body/eval_jaxpr/jit(_take)/gather | solution.py:35
  57.4 0.0 copy-done
  57.4 0.0 copy-start.1
  57.4 0.0 copy-start.2
  57.4 2.5 %convolution_bitcast_fusion.2 = f32[128,64,128]{2,0,1:T(8,128)S(1)} fusion(bf16[64,128,128]{2,1,0:T(8,128)(2,1)S(1)} %copy-done, bf16[64,128,128]{2,1,0:T(8,128)(2,1)} %gather_fusion, pred[64]{0:T(512)(128)(4,1)S(1)} %compare_and_fusion), kind=kOutput, calls=%fused_computation.10 | convolution fusion | flops 269484032 | bytes 8388672 | tf_op jit(solution)/shard_map/while/body/eval_jaxpr/tmk,mkn->tmn/dot_general | solution.py:36
  60.0 0.0 copy-done.1
  60.0 0.3 copy-done.2
  60.3 0.8 convolution_bitcast_fusion.1
  61.1 4.4 %fusion.14 = f32[128,8,128]{2,1,0:T(8,128)S(1)} fusion(f32[128,64,128]{2,0,1:T(8,128)S(1)} %convolution_bitcast_fusion.2, f32[64]{0:T(128)S(1)} %compare_convert_fusion, s32[64]{0:T(128)S(1)} %slice_bitcast_fusion), kind=kOutput, calls=%fused_computation.20 | convolution fusion | flops 100664320 | bytes 4719104 | tf_op jit(solution)/shard_map/while/body/eval_jaxpr/tmn,mh->thn/dot_general | solution.py:40
  65.4 4.4 %fusion.23 = bf16[128,8,128]{2,1,0:T(8,128)(2,1)S(1)} fusion(f32[128,64,128]{2,0,1:T(8,128)S(1)} %convolution_bitcast_fusion.1, f32[128,8,128]{2,1,0:T(8,128)S(1)} %fusion.14, f32[64]{0:T(128)S(1)} %compare_convert_fusion, s32[64]{0:T(128)S(1)} %slice_bitcast_fusion), kind=kOutput, calls=%fused_computation.23 | convolution fusion | flops 101450752 | bytes 4981248 | tf_op jit(solution)/shard_map/while/body/eval_jaxpr/tmn,mh->thn/dot_general | solution.py:43
  69.8 2.1 %gather_fusion.1 = bf16[64,128,128]{2,1,0:T(8,128)(2,1)} fusion(bf16[128,8,128]{2,0,1:T(8,128)(2,1)S(1)} %copy.29, s32[1024]{0:T(1024)S(1)} %pad_clamp_fusion), kind=kCustom, calls=%fused_computation.1 | custom fusion | bytes 4194560 | tf_op jit(solution)/shard_map/jit(_take)/gather | solution.py:49
  72.0 3.0 %convolution_bitcast_fusion = f32[128,64,128]{2,0,1:T(8,128)S(1)} fusion(bf16[64,128,128]{2,1,0:T(8,128)(2,1)} %param.10, bf16[64,128,128]{2,1,0:T(8,128)(2,1)} %gather_fusion.1, pred[64]{0:T(512)(128)(4,1)S(1)} %compare_and_fusion.1), kind=kOutput, calls=%fused_computation.8 | convolution fusion | flops 269484032 | bytes 8388672 | tf_op jit(solution)/shard_map/tmk,mkn->tmn/dot_general | solution.py:50
  74.9 6.0 %fusion.11 = f32[128,32,128]{2,1,0:T(8,128)} fusion(f32[128,64,128]{2,0,1:T(8,128)S(1)} %convolution_bitcast_fusion, f32[64]{0:T(128)S(1)} %compare_convert_fusion.1, s32[64]{0:T(128)S(1)} %slice_bitcast_fusion.1), kind=kOutput, calls=%fused_computation.19 | convolution fusion | flops 402657280 | bytes 6291968 | tf_op jit(solution)/shard_map/tmn,mo->ton/dot_general | solution.py:53
  81.0 2.7 %reshape.140 = f32[128,1,4096]{2,0,1:T(8,128)} reshape(f32[128,32,128]{2,1,0:T(8,128)} %fusion.11) | data formatting | bytes 4194304 | tf_op jit(solution)/shard_map/reshape | solution.py:54
  83.7 2.9 %copy.34 = f32[128,1,4096]{2,0,1:T(8,128)} copy(f32[128,1,4096]{0,2,1:T(8,128)} %bitcast.60) | data formatting | bytes 4194304 | tf_op jit(solution)/shard_map/mul | solution.py:54
  86.6 3.8 %add.85 = f32[128,1,4096]{2,0,1:T(8,128)} add(f32[128,1,4096]{2,0,1:T(8,128)} %reshape.140, f32[128,1,4096]{2,0,1:T(8,128)} %copy.34) | non-fusion elementwise | flops 524288 | bytes 6291456 | tf_op jit(solution)/shard_map/add | solution.py:54
  90.4 5.6 %copy.32 = f32[128,1,4096]{0,1,2:T(1,128)} copy(f32[128,1,4096]{2,0,1:T(8,128)} %add.85) | data formatting | bytes 4194304 | tf_op jit(solution)/shard_map/add | solution.py:54
  96.1 34.1 %all_to_all.17 = f32[128,1,4096]{0,1,2:T(1,128)} all-to-all(f32[128,1,4096]{0,1,2:T(1,128)} %copy.32), channel_id=1, replica_groups=mesh['ctx'=16,'tp'=16] {'ctx'}, dimensions={2} | all-to-all | bytes 4194304 | tf_op jit(solution)/shard_map/all_to_all | solution.py:55
  130.2 3.1 %copy.33 = f32[128,16,256]{2,1,0:T(8,128)} copy(f32[128,16,256]{0,2,1:T(8,128)} %bitcast.62) | data formatting | bytes 4194304 | tf_op jit(solution)/shard_map/all_to_all | solution.py:55
  133.3 0.0 reduce-scatter.2.cloned.1.call-update
  133.3 70.0 %reduce-scatter.2.cloned.1.call-done = f32[8,16,256]{2,1,0:T(8,128)} async-done(((f32[128,16,256]{2,1,0:T(8,128)}), f32[8,16,256]{2,1,0:T(8,128)}) %reduce-scatter.2.cloned.1.call-update) | async-done | bytes 131088 | tf_op jit(solution)/shard_map/reduce_scatter | solution.py:62
  203.3 1.5 convert_element_type.58
  (10 shorter events, 0.1 us)
Async XLA Ops:
  6.5 50.9 %copy-start = (bf16[64,128,128]{2,1,0:T(8,128)(2,1)S(1)}, bf16[64,128,128]{2,1,0:T(8,128)(2,1)}, u32[]{:S(2)}) copy-start(bf16[64,128,128]{2,1,0:T(8,128)(2,1)} %param.8) | copy-start | bytes 6291460
  6.5 11.9 %copy-start.3 = (s32[2,1]{0,1:T(1,128)S(1)}, s32[2,1]{0,1:T(1,128)}, u32[]{:S(2)}) copy-start(s32[2,1]{0,1:T(1,128)} %param.13) | copy-start | bytes 28
  6.5 13.8 %copy-start.4 = (s32[2,64]{1,0:T(2,128)S(1)}, s32[2,64]{1,0:T(2,128)}, u32[]{:S(2)}) copy-start(s32[2,64]{1,0:T(2,128)} %param.11) | copy-start | bytes 1540
  6.5 13.8 %copy-start.5 = (s32[2,64]{1,0:T(2,128)S(1)}, s32[2,64]{1,0:T(2,128)}, u32[]{:S(2)}) copy-start(s32[2,64]{1,0:T(2,128)} %param.12) | copy-start | bytes 1540
  8.8 38.3 %all-to-all-start = ((bf16[16,128,256]{1,2,0:T(8,128)(2,1)}), bf16[16,128,256]{1,2,0:T(8,128)(2,1)S(1)}, u32[]{:S(2)}, u32[]{:S(2)}) async-start(bf16[16,128,256]{1,2,0:T(8,128)(2,1)} %stack.2), calls=%async_computation | async-start | bytes 2097152 | tf_op jit(solution)/shard_map/all_to_all | solution.py:11
  18.4 184.9 %reduce-scatter.2.cloned.1.call-start = ((), (), s32[]{:S(2)}) async-start(), calls=%async_computation.3 | async-start | bytes 2228224 | tf_op jit(solution)/shard_map/reduce_scatter | solution.py:62
  57.4 2.5 %copy-start.1 = (bf16[64,128,128]{2,1,0:T(8,128)(2,1)S(1)}, bf16[64,128,128]{2,1,0:T(8,128)(2,1)}, u32[]{:S(2)}) copy-start(bf16[64,128,128]{2,1,0:T(8,128)(2,1)} %gather_fusion) | copy-start | bytes 6291460
  57.4 2.9 %copy-start.2 = (bf16[64,128,128]{2,1,0:T(8,128)(2,1)S(1)}, bf16[64,128,128]{2,1,0:T(8,128)(2,1)}, u32[]{:S(2)}) copy-start(bf16[64,128,128]{2,1,0:T(8,128)(2,1)} %param.9) | copy-start | bytes 6291460
Sparse Core Ops, SparseCore 0:
  133.5 69.8 reduce-scatter.1
